TPU v7x, 256 devices: a whole 4x4x8 slice. The times are simulated.
256 devices in a mesh: pb: 8 (over y, core), kv: 32 (over z, x).
Axes of the slice: x: 4, y: 4, z: 8, core: 2. Of those that a mesh axis runs over, the one named last changes fastest.
Arguments:
- queries: bfloat16 [65536, 4096], P(('pb', 'kv')), may hold values from -6 to 6
- keys: bfloat16 [8192, 4096], P(('pb', 'kv')), may hold values from -6 to 6
- values: bfloat16 [8192, 4096], P(('pb', 'kv')), may hold values from -6 to 6
- key_lists: int32 [512, 8], P('pb'), may hold values from 0 to 63, as said below
- counts: int32 [512], P('pb'), may hold values from 1 to 8, as said below
Outputs:
- attended: bfloat16 [65536, 4096], P(('pb', 'kv'))
Inputs may be any that keep to these rules, and one draw needn't show every extreme that they name: For every query block the first counts entries of its row of key_lists name different key blocks; entries past counts are valid block numbers that do not take part. `counts`: some query block uses all 8 entries of its list.
All inputs are finite; a program needn't handle non-finite values.
Results may differ from a plain program's by a relative error of at most 0.011.
Values may be sent and summed in bfloat16 or wider, within the bound.
No kernel may reach another device: no remote copies, remote signals or barrier semaphores. Data moves between devices by JAX's collectives and lax.ppermute only.
A program may use at most 64 MiB of HBM per device.

v0:
```python
import math
import jax
import jax.numpy as jnp
from jax import lax
from jax.sharding import PartitionSpec as P

HEADS = 32
HD = 128
BLK = 128
MOST = 8


def regroup(split_array, kv_count, pb_count):
    tokens_each = split_array.shape[0] // (kv_count * pb_count)
    shaped = split_array.reshape(kv_count, pb_count, tokens_each, split_array.shape[1])
    return shaped.transpose(1, 0, 2, 3).reshape(-1, split_array.shape[1])


def per_device(queries, keys, values, key_lists, counts):
    kv_count = lax.axis_size("kv")
    pb_count = lax.axis_size("pb")
    head_local = HEADS // kv_count
    scaling = HD ** (-0.5)
    key_whole, value_whole = (
        lax.all_gather(keys, "pb", axis=0, tiled=True),
        lax.all_gather(values, "pb", axis=0, tiled=True),
    )
    key_split, value_split = (
        lax.all_to_all(key_whole, "kv", split_axis=1, concat_axis=0, tiled=True),
        lax.all_to_all(value_whole, "kv", split_axis=1, concat_axis=0, tiled=True),
    )
    key_heads = regroup(key_split, kv_count, pb_count)
    value_heads = regroup(value_split, kv_count, pb_count)
    key_blocks = key_heads.reshape(-1, BLK, head_local, HD)
    value_blocks = value_heads.reshape(-1, BLK, head_local, HD)
    slot_of_key = jnp.arange(MOST * BLK, dtype=jnp.int32) // BLK

    def padded_group(item):
        group_queries, group_lists, group_counts = item
        members = group_queries.shape[0]
        listed_keys = key_blocks[group_lists].reshape(members, MOST * BLK, head_local, HD)
        listed_values = value_blocks[group_lists].reshape(members, MOST * BLK, head_local, HD)
        scores = (
            jnp.einsum(
                "gqhd,gkhd->ghqk", group_queries, listed_keys, preferred_element_type=jnp.float32
            )
            * scaling
        )
        usable = (slot_of_key[None, :] < group_counts[:, None])[:, None, None, :]
        largest = jnp.max(jnp.where(usable, scores, -jnp.inf), axis=-1, keepdims=True)
        raised = jnp.where(usable, jnp.exp(scores - largest), 0.0)
        totals = jnp.sum(raised, axis=-1, keepdims=True)
        weights = (raised / totals).astype(jnp.bfloat16)
        output = jnp.einsum(
            "ghqk,gkhd->gqhd", weights, listed_values, preferred_element_type=jnp.float32
        )
        return output.astype(jnp.bfloat16)

    query_blocks = queries.reshape(-1, BLK, queries.shape[1])
    exchanged = lax.all_to_all(query_blocks, "kv", split_axis=2, concat_axis=0, tiled=True)
    block_total = exchanged.shape[0]
    rows = exchanged.shape[1]
    per_group = math.gcd(block_total, max(1, 512 // rows))
    group_total = block_total // per_group
    grouped = exchanged.reshape(group_total, per_group, rows, head_local, HD)
    lists_grouped = key_lists.reshape(group_total, per_group, key_lists.shape[1])
    counts_grouped = counts.reshape(group_total, per_group)
    produced = lax.map(padded_group, (grouped, lists_grouped, counts_grouped))
    joined = produced.reshape(block_total, rows, head_local * HD)
    result = lax.all_to_all(joined, "kv", split_axis=0, concat_axis=2, tiled=True)
    return result.reshape(queries.shape)


def solution(mesh):
    return jax.shard_map(
        per_device,
        mesh=mesh,
        in_specs=(
            P(("pb", "kv"), None),
            P(("pb", "kv"), None),
            P(("pb", "kv"), None),
            P("pb", None),
            P("pb"),
        ),
        out_specs=P(("pb", "kv"), None),
        check_vma=False,
    )
```

profile of v0, /device:TPU:2, one launch (start us, length us, event | category | flops | bytes accessed | tf_op | source)
XLA Modules:
  0.0 411.0 jit_solution(12888155072686574849)
XLA Ops:
  6.5 6.2 %copy.31 = bf16[2,128,4096]{1,0,2:T(2,128)(2,1)} copy(bf16[2,128,4096]{2,1,0:T(8,128)(2,1)} %bitcast.84) | data formatting | bytes 4194304 | tf_op jit(solution)/shard_map/reshape | solution.py:59
  12.7 11.6 %all-to-all-start.1 = ((bf16[2,128,4096]{1,0,2:T(2,128)(2,1)}), bf16[2,128,4096]{1,0,2:T(2,128)(2,1)S(1)}, u32[]{:S(2)}, u32[]{:S(2)}) async-start(bf16[2,128,4096]{1,0,2:T(2,128)(2,1)} %copy.31), calls=%async_computation.1 | async-start | bytes 4194304 | tf_op jit(solution)/shard_map/all_to_all | solution.py:60
  25.1 30.8 %all-gather.5.cloned.1.call-done = bf16[256,4096]{1,0:T(8,128)(2,1)} async-done(((bf16[32,4096]{1,0:T(8,128)(2,1)}), bf16[256,4096]{1,0:T(8,128)(2,1)}) %all-gather.5.cloned.1.call-update) | async-done | bytes 2097168 | tf_op jit(solution)/shard_map/all_gather | solution.py:25
  55.9 4.1 copy.34
  60.0 13.6 %all-to-all-done.1 = bf16[2,128,4096]{1,0,2:T(2,128)(2,1)S(1)} async-done(((bf16[2,128,4096]{1,0,2:T(2,128)(2,1)}), bf16[2,128,4096]{1,0,2:T(2,128)(2,1)S(1)}, u32[]{:S(2)}, u32[]{:S(2)}) %all-to-all-start.1) | async-done | bytes 2097184 | tf_op jit(solution)/shard_map/all_to_all | solution.py:60
  73.6 6.9 %all-to-all-start.2 = ((bf16[256,32,128]{0,2,1:T(8,128)(2,1)}), bf16[256,32,128]{0,2,1:T(8,128)(2,1)}, u32[]{:S(2)}, u32[]{:S(2)}) async-start(bf16[256,32,128]{0,2,1:T(8,128)(2,1)} %bitcast.76), calls=%async_computation.2 | async-start | bytes 4194304 | tf_op jit(solution)/shard_map/all_to_all | solution.py:29
  81.2 30.8 %all-gather.3.cloned.1.call-done = bf16[256,4096]{1,0:T(8,128)(2,1)} async-done(((bf16[32,4096]{1,0:T(8,128)(2,1)}), bf16[256,4096]{1,0:T(8,128)(2,1)}) %all-gather.3.cloned.1.call-update) | async-done | bytes 2097168 | tf_op jit(solution)/shard_map/all_gather | solution.py:26
  112.1 4.1 copy.28
  116.1 12.9 %all-to-all-done.2 = bf16[256,32,128]{0,2,1:T(8,128)(2,1)} async-done(((bf16[256,32,128]{0,2,1:T(8,128)(2,1)}), bf16[256,32,128]{0,2,1:T(8,128)(2,1)}, u32[]{:S(2)}, u32[]{:S(2)}) %all-to-all-start.2) | async-done | bytes 2097184 | tf_op jit(solution)/shard_map/all_to_all | solution.py:29
  129.1 6.7 %all-to-all-start = ((bf16[256,32,128]{0,2,1:T(8,128)(2,1)}), bf16[256,32,128]{0,2,1:T(8,128)(2,1)}, u32[]{:S(2)}, u32[]{:S(2)}) async-start(bf16[256,32,128]{0,2,1:T(8,128)(2,1)} %bitcast.77), calls=%async_computation | async-start | bytes 4194304 | tf_op jit(solution)/shard_map/all_to_all | solution.py:30
  137.7 4.1 copy.33
  141.7 4.1 copy.35
  147.8 37.0 %all-to-all-done = bf16[256,32,128]{0,2,1:T(8,128)(2,1)} async-done(((bf16[256,32,128]{0,2,1:T(8,128)(2,1)}), bf16[256,32,128]{0,2,1:T(8,128)(2,1)}, u32[]{:S(2)}, u32[]{:S(2)}) %all-to-all-start) | async-done | bytes 2097184 | tf_op jit(solution)/shard_map/all_to_all | solution.py:30
  184.8 4.1 copy.29
  188.9 3.4 copy.30
  192.2 154.8 %while.11 = (s32[]{:T(128)}, bf16[16,4,128,1,128]{4,2,1,0,3:T(8,128)(2,1)}, s32[16,4,8]{2,1,0:T(4,128)S(1)}, bf16[64,128,1,128]{3,1,0,2:T(8,128)(2,1)}, s32[16,4...) while((s32[]{:T(128)}, ...), condition=%wide.region_3.4_spmd.clone, body=%wide.region_0.3_spmd.clone.sunk | while | flops 272709728 | bytes 15493133 | solution.py:68
  196.5 2.3 gather_fusion
  206.2 2.3 gather_fusion
  244.9 2.3 gather_fusion
  254.6 2.3 gather_fusion
  264.3 2.3 gather_fusion
  293.3 2.3 gather_fusion
  302.9 2.3 gather_fusion
  347.0 53.5 %all_to_all.62 = bf16[64,128,128]{2,1,0:T(8,128)(2,1)S(1)} all-to-all(bf16[64,128,128]{2,1,0:T(8,128)(2,1)} %bitcast.85), channel_id=1, replica_groups=mesh['pb'=8,'kv'=32] {'kv'}, dimensions={0} | all-to-all | bytes 4194304 | tf_op jit(solution)/shard_map/all_to_all | solution.py:70
  (216 shorter events, 146.6 us)
Async XLA Ops:
  12.7 60.9 %all-to-all-start.1 = ((bf16[2,128,4096]{1,0,2:T(2,128)(2,1)}), bf16[2,128,4096]{1,0,2:T(2,128)(2,1)S(1)}, u32[]{:S(2)}, u32[]{:S(2)}) async-start(bf16[2,128,4096]{1,0,2:T(2,128)(2,1)} %copy.31), calls=%async_computation.1 | async-start | bytes 4194304 | tf_op jit(solution)/shard_map/all_to_all | solution.py:60
  24.3 31.6 %all-gather.5.cloned.1.call-start = ((), (), s32[]{:S(2)}) async-start(), calls=%async_computation.5 | async-start | bytes 2359296 | tf_op jit(solution)/shard_map/all_gather | solution.py:25
  73.6 55.5 %all-to-all-start.2 = ((bf16[256,32,128]{0,2,1:T(8,128)(2,1)}), bf16[256,32,128]{0,2,1:T(8,128)(2,1)}, u32[]{:S(2)}, u32[]{:S(2)}) async-start(bf16[256,32,128]{0,2,1:T(8,128)(2,1)} %bitcast.76), calls=%async_computation.2 | async-start | bytes 4194304 | tf_op jit(solution)/shard_map/all_to_all | solution.py:29
  80.5 31.6 %all-gather.3.cloned.1.call-start = ((), (), s32[]{:S(2)}) async-start(), calls=%async_computation.4 | async-start | bytes 2359296 | tf_op jit(solution)/shard_map/all_gather | solution.py:26
  129.1 6.8 %copy-start = (s32[64,8]{0,1:T(8,128)S(1)}, s32[64,8]{0,1:T(8,128)}, u32[]{:S(2)}) copy-start(s32[64,8]{0,1:T(8,128)} %param.10) | copy-start | bytes 6148
  129.1 6.9 %copy-start.1 = (s32[64]{0:T(128)S(1)}, s32[64]{0:T(128)}, u32[]{:S(2)}) copy-start(s32[64]{0:T(128)} %param.11) | copy-start | bytes 772
  129.1 55.7 %all-to-all-start = ((bf16[256,32,128]{0,2,1:T(8,128)(2,1)}), bf16[256,32,128]{0,2,1:T(8,128)(2,1)}, u32[]{:S(2)}, u32[]{:S(2)}) async-start(bf16[256,32,128]{0,2,1:T(8,128)(2,1)} %bitcast.77), calls=%async_computation | async-start | bytes 4194304 | tf_op jit(solution)/shard_map/all_to_all | solution.py:30
Sparse Core Ops, SparseCore 0:
  27.0 28.8 all-gather.4
  83.2 28.8 all-gather.2
where the time goes:
time: 413 us; the launch traced here: 411 us
  waiting for transfers between devices  127 us (31%)
  local copies, waits for them, and re-layouts  101 us (24%)
  matrix products  56.6 us (14%)
  blocking collectives  53.5 us (13%)
  other arithmetic  33.6 us (8%)
  starting transfers between devices  25.4 us (6%)
  between operations  13.5 us (3%)
    all_to_all x1, blocking collectives, per_device(): lax.all_to_all(joined, 'kv', split_axis=0, concat_axis=2, tiled=True)  53.5 us
    gather x16, local copies, waits for them, and re-layouts, padded_group(): value_blocks[group_lists].reshape(members, MOST * BLK, head_local, HD)  37.4 us
    all_to_all x1, waiting for transfers between devices, per_device(): lax.all_to_all(value_whole, 'kv', split_axis=1, concat_axis=0, tiled=True)  37 us
    dot_general x16, matrix products, padded_group(): jnp.einsum('ghqk,gkhd->gqhd', weights, listed_values, preferred_element_t...  35.1 us
    sub x16, other arithmetic, padded_group(): raised = jnp.where(usable, jnp.exp(scores - largest), 0.0)  32.1 us
    all_gather x1, waiting for transfers between devices, per_device(): lax.all_gather(keys, 'pb', axis=0, tiled=True)  30.8 us
    all_gather x1, waiting for transfers between devices, per_device(): lax.all_gather(values, 'pb', axis=0, tiled=True)  30.8 us
    dot_general x16, matrix products, padded_group(): jnp.einsum('gqhd,gkhd->ghqk', group_queries, listed_keys, preferred_eleme...  21.5 us
  transfers between devices with their start and end apart: 5, of which 5 were waited for; matrix products, arithmetic and copies ran while one was open for 5% of the time, Pallas kernels for 0%

commit v1 on v0

--- a/solution.py
+++ b/solution.py
@@ -8,6 +8,22 @@
 HD = 128
 BLK = 128
 MOST = 8
+
+
+def ring_gather(x, axis, dim):
+    ways, here, step = (lax.axis_size(axis), lax.axis_index(axis), x.shape[dim])
+    dims = [n * ways if d == dim else n for d, n in enumerate(x.shape)]
+    full = lax.dynamic_update_slice_in_dim(jnp.zeros(dims, x.dtype), x, here * step, axis=dim)
+    going_up = going_down = x
+    for far in range(1, ways // 2 + 1):
+        going_up = lax.ppermute(going_up, axis, [(d, (d + 1) % ways) for d in range(ways)])
+        full = lax.dynamic_update_slice_in_dim(full, going_up, (here - far) % ways * step, axis=dim)
+        if 2 * far < ways:
+            going_down = lax.ppermute(going_down, axis, [(d, (d - 1) % ways) for d in range(ways)])
+            full = lax.dynamic_update_slice_in_dim(
+                full, going_down, (here + far) % ways * step, axis=dim
+            )
+    return full
 
 
 def regroup(split_array, kv_count, pb_count):
@@ -22,7 +38,7 @@
     head_local = HEADS // kv_count
     scaling = HD ** (-0.5)
     key_whole, value_whole = (
-        lax.all_gather(keys, "pb", axis=0, tiled=True),
+        ring_gather(keys, "pb", 0),
         lax.all_gather(values, "pb", axis=0, tiled=True),
     )
     key_split, value_split = (

time: 413 us -> 492 us (1.19); the launches traced: 411 us -> 483 us
  local copies, waits for them, and re-layouts: 101 us -> 196 us
  waiting for transfers between devices: 127 us -> 90.1 us
  starting transfers between devices: 25.4 us -> 37.5 us
    dynamic_update_slice x0 -> x8, local copies, waits for them, and re-layouts: none -> 88.2 us  [the longest x4 42.6 us: ring_gather(): lax.dynamic_update_slice_in_dim(full, going_up, (here - far) % ways * ste...]
    all_gather x1 -> x0, waiting for transfers between devices: 30.8 us -> none  [per_device(): lax.all_gather(keys, 'pb', axis=0, tiled=True)]
    all_to_all x1, waiting for transfers between devices: 13.6 us -> 0.01 us  [per_device(): lax.all_to_all(query_blocks, 'kv', split_axis=2, concat_axis=0, tiled=True)]
    ppermute x0 -> x7, waiting for transfers between devices: none -> 11 us  [the longest x4 10.2 us: ring_gather(): lax.ppermute(going_up, axis, [(d, (d + 1) % ways) for d in range(ways)])]
    ppermute x0 -> x7, starting transfers between devices: none -> 9.4 us  [the longest x3 9.38 us: ring_gather(): lax.ppermute(going_down, axis, [(d, (d - 1) % ways) for d in range(ways)])]
    ppermute x0 -> x7, local copies, waits for them, and re-layouts: none -> 8.11 us  [the longest x4 4.79 us: ring_gather(): lax.ppermute(going_up, axis, [(d, (d + 1) % ways) for d in range(ways)])]
  transfers between devices with their start and end apart: 5 -> 11, of which waited for: 5 -> 7; matrix products, arithmetic and copies ran while one was open for 5% -> 24% of each run, Pallas kernels for 0% -> 0%
where the time goes in v1:
time: 492 us; the launch traced here: 483 us
  local copies, waits for them, and re-layouts  196 us (40%)
  waiting for transfers between devices  90.1 us (18%)
  matrix products  56.6 us (12%)
  blocking collectives  54 us (11%)
  starting transfers between devices  37.5 us (8%)
  other arithmetic  34 us (7%)
  between operations  13.7 us (3%)
    all_to_all x1, blocking collectives, per_device(): lax.all_to_all(joined, 'kv', split_axis=0, concat_axis=2, tiled=True)  54 us
    dynamic_update_slice x4, local copies, waits for them, and re-layouts, ring_gather(): lax.dynamic_update_slice_in_dim(full, going_up, (here - far) % ways * ste...  42.6 us
    gather x16, local copies, waits for them, and re-layouts, padded_group(): value_blocks[group_lists].reshape(members, MOST * BLK, head_local, HD)  37.4 us
    dynamic_update_slice x3, local copies, waits for them, and re-layouts, ring_gather(): lax.dynamic_update_slice_in_dim(full, going_down, (here + far) % ways * s...  35.3 us
    all_to_all x1, waiting for transfers between devices, per_device(): lax.all_to_all(value_whole, 'kv', split_axis=1, concat_axis=0, tiled=True)  35.2 us
    dot_general x16, matrix products, padded_group(): jnp.einsum('ghqk,gkhd->gqhd', weights, listed_values, preferred_element_t...  35.1 us
    sub x16, other arithmetic, padded_group(): raised = jnp.where(usable, jnp.exp(scores - largest), 0.0)  32.5 us
    all_gather x1, waiting for transfers between devices, per_device(): lax.all_gather(values, 'pb', axis=0, tiled=True)  30.1 us
  transfers between devices with their start and end apart: 11, of which 7 were waited for; matrix products, arithmetic and copies ran while one was open for 24% of the time, Pallas kernels for 0%

profile of v1, /device:TPU:2, one launch (start us, length us, event | category | flops | bytes accessed | tf_op | source)
XLA Modules:
  0.0 482.8 jit_solution(17842264662182303300)
XLA Ops:
  6.5 6.2 %copy.33 = bf16[2,128,4096]{1,0,2:T(2,128)(2,1)} copy(bf16[2,128,4096]{2,1,0:T(8,128)(2,1)} %bitcast.84) | data formatting | bytes 4194304 | tf_op jit(solution)/shard_map/reshape | solution.py:75
  12.7 11.7 %all-to-all-start.1 = ((bf16[2,128,4096]{1,0,2:T(2,128)(2,1)}), bf16[2,128,4096]{1,0,2:T(2,128)(2,1)S(1)}, u32[]{:S(2)}, u32[]{:S(2)}) async-start(bf16[2,128,4096]{1,0,2:T(2,128)(2,1)} %copy.33), calls=%async_computation.1 | async-start | bytes 4194304 | tf_op jit(solution)/shard_map/all_to_all | solution.py:76
  27.4 4.1 collective-permute-done
  39.3 3.2 collective-permute-start.5
  47.7 10.2 %dynamic_update_slice.28 = bf16[256,4096]{0,1:T(8,128)(2,1)} dynamic-update-slice(bf16[256,4096]{0,1:T(8,128)(2,1)} %broadcast_in_dim.36, bf16[32,4096]{0,1:T(8,128)(2,1)S(1)} %copy.36, s32[]{:T(128)S(6)} %select_n.81, s32[]{:T(128)} %copy.73) | dynamic-update-slice | bytes 524292 | tf_op jit(solution)/shard_map/dynamic_update_slice | solution.py:16
  59.4 11.1 %dynamic_update_slice.29 = bf16[256,4096]{0,1:T(8,128)(2,1)} dynamic-update-slice(bf16[256,4096]{0,1:T(8,128)(2,1)} %dynamic_update_slice.28, bf16[32,4096]{0,1:T(8,128)(2,1)S(1)} %copy.37, s32[]{:T(128)S(6)} %select_n.83, s32[]{:T(128)} %copy.73) | dynamic-update-slice | bytes 524292 | tf_op jit(solution)/shard_map/dynamic_update_slice | solution.py:20
  71.0 11.8 %dynamic_update_slice.30 = bf16[256,4096]{0,1:T(8,128)(2,1)} dynamic-update-slice(bf16[256,4096]{0,1:T(8,128)(2,1)} %dynamic_update_slice.29, bf16[32,4096]{0,1:T(8,128)(2,1)S(1)} %copy.38, s32[]{:T(128)S(6)} %select_n.85, s32[]{:T(128)} %copy.73) | dynamic-update-slice | bytes 524292 | tf_op jit(solution)/shard_map/dynamic_update_slice | solution.py:23
  83.3 11.1 %dynamic_update_slice.31 = bf16[256,4096]{0,1:T(8,128)(2,1)} dynamic-update-slice(bf16[256,4096]{0,1:T(8,128)(2,1)} %dynamic_update_slice.30, bf16[32,4096]{0,1:T(8,128)(2,1)S(1)} %copy.39, s32[]{:T(128)S(6)} %select_n.87, s32[]{:T(128)} %copy.73) | dynamic-update-slice | bytes 524292 | tf_op jit(solution)/shard_map/dynamic_update_slice | solution.py:20
  95.8 11.8 %dynamic_update_slice.32 = bf16[256,4096]{0,1:T(8,128)(2,1)} dynamic-update-slice(bf16[256,4096]{0,1:T(8,128)(2,1)} %dynamic_update_slice.31, bf16[32,4096]{0,1:T(8,128)(2,1)S(1)} %copy.40, s32[]{:T(128)S(6)} %select_n.89, s32[]{:T(128)} %copy.73) | dynamic-update-slice | bytes 524292 | tf_op jit(solution)/shard_map/dynamic_update_slice | solution.py:23
  109.0 11.1 %dynamic_update_slice.33 = bf16[256,4096]{0,1:T(8,128)(2,1)} dynamic-update-slice(bf16[256,4096]{0,1:T(8,128)(2,1)} %dynamic_update_slice.32, bf16[32,4096]{0,1:T(8,128)(2,1)S(1)} %copy.41, s32[]{:T(128)S(6)} %select_n.91, s32[]{:T(128)} %copy.73) | dynamic-update-slice | bytes 524292 | tf_op jit(solution)/shard_map/dynamic_update_slice | solution.py:20
  121.5 11.8 %dynamic_update_slice.34 = bf16[256,4096]{0,1:T(8,128)(2,1)} dynamic-update-slice(bf16[256,4096]{0,1:T(8,128)(2,1)} %dynamic_update_slice.33, bf16[32,4096]{0,1:T(8,128)(2,1)S(1)} %copy.42, s32[]{:T(128)S(6)} %select_n.93, s32[]{:T(128)} %copy.73) | dynamic-update-slice | bytes 524292 | tf_op jit(solution)/shard_map/dynamic_update_slice | solution.py:23
  134.7 9.4 %dynamic_update_slice.35 = bf16[256,4096]{0,1:T(8,128)(2,1)} dynamic-update-slice(bf16[256,4096]{0,1:T(8,128)(2,1)} %dynamic_update_slice.34, bf16[32,4096]{0,1:T(8,128)(2,1)S(1)} %copy.43, s32[]{:T(128)S(6)} %select_n.95, s32[]{:T(128)} %copy.73) | dynamic-update-slice | bytes 524292 | tf_op jit(solution)/shard_map/dynamic_update_slice | solution.py:20
  144.1 9.8 %all-to-all-start.2 = ((bf16[256,32,128]{0,2,1:T(8,128)(2,1)}), bf16[256,32,128]{0,2,1:T(8,128)(2,1)}, u32[]{:S(2)}, u32[]{:S(2)}) async-start(bf16[256,32,128]{0,2,1:T(8,128)(2,1)} %bitcast.77), calls=%async_computation.2 | async-start | bytes 4194304 | tf_op jit(solution)/shard_map/all_to_all | solution.py:45
  154.6 30.1 %all-gather.2.cloned.1.call-done = bf16[256,4096]{1,0:T(8,128)(2,1)} async-done(((bf16[32,4096]{1,0:T(8,128)(2,1)}), bf16[256,4096]{1,0:T(8,128)(2,1)}) %all-gather.2.cloned.1.call-update) | async-done | bytes 2097168 | tf_op jit(solution)/shard_map/all_gather | solution.py:42
  184.7 4.1 copy.30
  188.8 13.2 %all-to-all-done.2 = bf16[256,32,128]{0,2,1:T(8,128)(2,1)} async-done(((bf16[256,32,128]{0,2,1:T(8,128)(2,1)}), bf16[256,32,128]{0,2,1:T(8,128)(2,1)}, u32[]{:S(2)}, u32[]{:S(2)}) %all-to-all-start.2) | async-done | bytes 2097184 | tf_op jit(solution)/shard_map/all_to_all | solution.py:45
  202.0 6.5 %all-to-all-start = ((bf16[256,32,128]{0,2,1:T(8,128)(2,1)}), bf16[256,32,128]{0,2,1:T(8,128)(2,1)}, u32[]{:S(2)}, u32[]{:S(2)}) async-start(bf16[256,32,128]{0,2,1:T(8,128)(2,1)} %bitcast.76), calls=%async_computation | async-start | bytes 4194304 | tf_op jit(solution)/shard_map/all_to_all | solution.py:46
  210.3 4.1 copy.35
  214.4 4.1 copy.44
  220.6 35.2 %all-to-all-done = bf16[256,32,128]{0,2,1:T(8,128)(2,1)} async-done(((bf16[256,32,128]{0,2,1:T(8,128)(2,1)}), bf16[256,32,128]{0,2,1:T(8,128)(2,1)}, u32[]{:S(2)}, u32[]{:S(2)}) %all-to-all-start) | async-done | bytes 2097184 | tf_op jit(solution)/shard_map/all_to_all | solution.py:46
  255.7 4.1 copy.31
  259.8 3.3 copy.32
  263.1 155.1 %while.11 = (s32[]{:T(128)}, bf16[16,4,128,1,128]{4,2,1,0,3:T(8,128)(2,1)}, s32[16,4,8]{2,1,0:T(4,128)S(1)}, bf16[64,128,1,128]{3,1,0,2:T(8,128)(2,1)}, s32[16,4...) while((s32[]{:T(128)}, ...), condition=%wide.region_3.4_spmd.clone, body=%wide.region_0.3_spmd.clone.sunk | while | flops 272709728 | bytes 15493133 | solution.py:84
  418.3 54.0 %all_to_all.62 = bf16[64,128,128]{2,1,0:T(8,128)(2,1)S(1)} all-to-all(bf16[64,128,128]{2,1,0:T(8,128)(2,1)} %bitcast.85), channel_id=1, replica_groups=mesh['pb'=8,'kv'=32] {'kv'}, dimensions={0} | all-to-all | bytes 4194304 | tf_op jit(solution)/shard_map/all_to_all | solution.py:86
  (255 shorter events, 186.6 us)
Async XLA Ops:
  12.7 11.8 %copy-start = (bf16[32,4096]{1,0:T(8,128)(2,1)S(1)}, bf16[32,4096]{1,0:T(8,128)(2,1)}, u32[]{:S(2)}) copy-start(bf16[32,4096]{1,0:T(8,128)(2,1)} %param.8) | copy-start | bytes 786436
  12.7 131.4 %all-to-all-start.1 = ((bf16[2,128,4096]{1,0,2:T(2,128)(2,1)}), bf16[2,128,4096]{1,0,2:T(2,128)(2,1)S(1)}, u32[]{:S(2)}, u32[]{:S(2)}) async-start(bf16[2,128,4096]{1,0,2:T(2,128)(2,1)} %copy.33), calls=%async_computation.1 | async-start | bytes 4194304 | tf_op jit(solution)/shard_map/all_to_all | solution.py:76
  24.5 7.0 %collective-permute-start = (bf16[32,4096]{1,0:T(8,128)(2,1)S(1)}, bf16[32,4096]{1,0:T(8,128)(2,1)S(1)}, u32[]{:S(2)}, u32[]{:S(2)}) collective-permute-start(bf16[32,4096]{1,0:T(8,128)(2,1)S(1)} %copy-done), channel_id=1, source_target_pairs={{0,32},{32,64},{64,96},{96,128},{128,160},{160,192},{192,224},{224... | collective-permute-start | bytes 786440 | tf_op jit(solution)/shard_map/ppermute | solution.py:19
  24.5 7.0 %collective-permute-start.1 = (bf16[32,4096]{1,0:T(8,128)(2,1)S(1)}, bf16[32,4096]{1,0:T(8,128)(2,1)S(1)}, u32[]{:S(2)}, u32[]{:S(2)}) collective-permute-start(bf16[32,4096]{1,0:T(8,128)(2,1)S(1)} %copy-done), channel_id=1, source_target_pairs={{0,224},{32,0},{64,32},{96,64},{128,96},{160,128},{192,160},{224,1... | collective-permute-start | bytes 786440 | tf_op jit(solution)/shard_map/ppermute | solution.py:22
  31.5 14.1 %copy-start.5 = (bf16[32,4096]{1,0:T(8,128)(2,1)}, bf16[32,4096]{1,0:T(8,128)(2,1)S(1)}, u32[]{:S(2)}) copy-start(bf16[32,4096]{1,0:T(8,128)(2,1)S(1)} %collective-permute-done) | copy-start | bytes 786436
  31.5 7.0 %collective-permute-start.2 = (bf16[32,4096]{1,0:T(8,128)(2,1)S(1)}, bf16[32,4096]{1,0:T(8,128)(2,1)S(1)}, u32[]{:S(2)}, u32[]{:S(2)}) collective-permute-start(bf16[32,4096]{1,0:T(8,128)(2,1)S(1)} %collective-permute-done), channel_id=1, source_target_pairs={{0,32},{32,64},{64,96},{96,128},{128,160},{160,192},{192,224},{224... | collective-permute-start | bytes 786440 | tf_op jit(solution)/shard_map/ppermute | solution.py:19
  31.5 0.7 copy-start.1
  32.2 7.1 %collective-permute-start.3 = (bf16[32,4096]{1,0:T(8,128)(2,1)S(1)}, bf16[32,4096]{1,0:T(8,128)(2,1)}, u32[]{:S(2)}, u32[]{:S(2)}) collective-permute-start(bf16[32,4096]{1,0:T(8,128)(2,1)S(1)} %collective-permute-done.1), channel_id=1, source_target_pairs={{0,224},{32,0},{64,32},{96,64},{128,96},{160,128},{192,160},{224,1... | collective-permute-start | bytes 786440 | tf_op jit(solution)/shard_map/ppermute | solution.py:22
  38.5 0.8 copy-start.3
  38.5 7.1 %collective-permute-start.4 = (bf16[32,4096]{1,0:T(8,128)(2,1)S(1)}, bf16[32,4096]{1,0:T(8,128)(2,1)}, u32[]{:S(2)}, u32[]{:S(2)}) collective-permute-start(bf16[32,4096]{1,0:T(8,128)(2,1)S(1)} %collective-permute-done.2), channel_id=1, source_target_pairs={{0,32},{32,64},{64,96},{96,128},{128,160},{160,192},{192,224},{224... | collective-permute-start | bytes 786440 | tf_op jit(solution)/shard_map/ppermute | solution.py:19
  39.3 80.7 %collective-permute-start.5 = (bf16[32,4096]{1,0:T(8,128)(2,1)}, bf16[32,4096]{1,0:T(8,128)(2,1)}, u32[]{:S(2)}, u32[]{:S(2)}) collective-permute-start(bf16[32,4096]{1,0:T(8,128)(2,1)} %collective-permute-done.3), channel_id=1, source_target_pairs={{0,224},{32,0},{64,32},{96,64},{128,96},{160,128},{192,160},{224,1... | collective-permute-start | bytes 786440 | tf_op jit(solution)/shard_map/ppermute | solution.py:22
  45.6 87.6 %collective-permute-start.6 = (bf16[32,4096]{1,0:T(8,128)(2,1)}, bf16[32,4096]{1,0:T(8,128)(2,1)}, u32[]{:S(2)}, u32[]{:S(2)}) collective-permute-start(bf16[32,4096]{1,0:T(8,128)(2,1)} %collective-permute-done.4), channel_id=1, source_target_pairs={{0,32},{32,64},{64,96},{96,128},{128,160},{160,192},{192,224},{224... | collective-permute-start | bytes 786440 | tf_op jit(solution)/shard_map/ppermute | solution.py:19
  58.0 12.5 %copy-start.2 = (bf16[32,4096]{1,0:T(8,128)(2,1)S(1)}, bf16[32,4096]{1,0:T(8,128)(2,1)}, u32[]{:S(2)}) copy-start(bf16[32,4096]{1,0:T(8,128)(2,1)} %copy-done.1) | copy-start | bytes 786436
  71.0 11.8 %copy-start.4 = (bf16[32,4096]{1,0:T(8,128)(2,1)S(1)}, bf16[32,4096]{1,0:T(8,128)(2,1)}, u32[]{:S(2)}) copy-start(bf16[32,4096]{1,0:T(8,128)(2,1)} %copy-done.3) | copy-start | bytes 786436
  144.1 58.0 %all-to-all-start.2 = ((bf16[256,32,128]{0,2,1:T(8,128)(2,1)}), bf16[256,32,128]{0,2,1:T(8,128)(2,1)}, u32[]{:S(2)}, u32[]{:S(2)}) async-start(bf16[256,32,128]{0,2,1:T(8,128)(2,1)} %bitcast.77), calls=%async_computation.2 | async-start | bytes 4194304 | tf_op jit(solution)/shard_map/all_to_all | solution.py:45
  153.9 30.8 %all-gather.2.cloned.1.call-start = ((), (), s32[]{:S(2)}) async-start(), calls=%async_computation.4 | async-start | bytes 2359296 | tf_op jit(solution)/shard_map/all_gather | solution.py:42
  202.0 6.5 %copy-start.6 = (s32[64,8]{0,1:T(8,128)S(1)}, s32[64,8]{0,1:T(8,128)}, u32[]{:S(2)}) copy-start(s32[64,8]{0,1:T(8,128)} %param.10) | copy-start | bytes 6148
  202.0 6.6 %copy-start.7 = (s32[64]{0:T(128)S(1)}, s32[64]{0:T(128)}, u32[]{:S(2)}) copy-start(s32[64]{0:T(128)} %param.11) | copy-start | bytes 772
  202.0 53.7 %all-to-all-start = ((bf16[256,32,128]{0,2,1:T(8,128)(2,1)}), bf16[256,32,128]{0,2,1:T(8,128)(2,1)}, u32[]{:S(2)}, u32[]{:S(2)}) async-start(bf16[256,32,128]{0,2,1:T(8,128)(2,1)} %bitcast.76), calls=%async_computation | async-start | bytes 4194304 | tf_op jit(solution)/shard_map/all_to_all | solution.py:46
Sparse Core Ops, SparseCore 0:
  156.6 28.0 all-gather.1
